TPU v7x, 256 devices: a whole 4x4x8 slice. The times are simulated.
256 devices in a mesh: ch: 64 (over z_lo, y, x), ta: 4 (over z_hi, core).
Axes of the slice: x: 4, y: 4, z: 8 (z_hi: 2, z_lo: 4; z = z_hi * 4 + z_lo), core: 2. Of those that a mesh axis runs over, the one named last changes fastest.
Arguments:
- raw: bfloat16 [16384, 20480], P('ch', 'ta'), may hold values from -40 to 40
- fir_taps: bfloat16 [129], replicated, may hold values from -0.5 to 0.5
- start_basis: float32 [512, 16], replicated, may hold values from -6 to 6
Outputs:
- cleaned: bfloat16 [16384, 20480], P('ch', 'ta')
All inputs are finite; a program needn't handle non-finite values.
Results may differ from a plain program's by a relative error of at most 0.008.
Values may be sent and summed in bfloat16 or wider, within the bound.
No kernel may reach another device: no remote copies, remote signals or barrier semaphores. Data moves between devices by JAX's collectives and lax.ppermute only.
A program may use at most 64 MiB of HBM per device.

v0:
```python
import math
import jax
import jax.numpy as jnp
from jax import lax
from jax.sharding import PartitionSpec as P

TAPS = 129
GAUGE = 4
STRIDE = 128
RANK = 16
ITERS = 6
WIN = 512


def with_halo(block, sides, width):
    for axis, dim in sides:
        count = lax.axis_size(axis)
        forward = [(i, i + 1) for i in range(count - 1)]
        backward = [(target, source) for source, target in forward]
        low = lax.ppermute(
            lax.slice_in_dim(block, block.shape[dim] - width, None, axis=dim), axis, forward
        )
        high = lax.ppermute(lax.slice_in_dim(block, 0, width, axis=dim), axis, backward)
        block = jnp.concatenate([low, block, high], axis=dim)
    return block


def shifted(value, axis, steps):
    count = lax.axis_size(axis)
    first, last = (max(0, -steps), min(count, count - steps))
    return lax.ppermute(value, axis, [(source, source + steps) for source in range(first, last)])


def toeplitz_band(taps, width):
    count = taps.shape[0]
    line = jnp.concatenate([taps, jnp.zeros((width,), taps.dtype)])
    flat = jnp.tile(line, width)[: width * (count + width - 1)]
    return flat.reshape(width, count + width - 1).T


def orthonormal(image):
    gram = jnp.einsum("wcr,wcs->wrs", image, image, precision=lax.Precision.HIGHEST)
    lower = jnp.linalg.cholesky(gram)
    return lax.linalg.triangular_solve(lower, image, left_side=False, lower=True, transpose_a=True)


def per_device(raw, fir_taps, start_basis):
    chans = raw.shape[0]
    samples = raw.shape[1]
    half = (TAPS - 1) // 2
    width = math.gcd(samples, 256)
    padded = with_halo(raw, (("ta", 1),), half)
    band_matrix = toeplitz_band(fir_taps, width)
    pieces = jnp.stack(
        [
            padded[:, number * width : number * width + width + TAPS - 1]
            for number in range(samples // width)
        ]
    )
    filtered = jnp.einsum(
        "bct,tu->cbu", pieces, band_matrix, preferred_element_type=jnp.float32
    ).reshape(chans, samples)
    extended = with_halo(filtered, (("ch", 0),), GAUGE)
    gauged = (extended[2 * GAUGE :] - extended[: -2 * GAUGE]).astype(jnp.bfloat16)
    lower_part = shifted(gauged, "ch", 1)
    upper_part = shifted(gauged[:STRIDE], "ch", -1)
    stacked = jnp.concatenate([lower_part, gauged, upper_part], axis=0)
    windows = chans // STRIDE
    total_time = samples * lax.axis_size("ta")
    basis = jnp.broadcast_to(start_basis, (windows, WIN, RANK))
    partial_mats = jnp.stack(
        [
            jnp.dot(
                stacked[number * STRIDE : number * STRIDE + WIN],
                stacked[number * STRIDE : number * STRIDE + WIN].T,
                preferred_element_type=jnp.float32,
            )
            for number in range(windows)
        ]
    )
    scatter_mat = lax.psum(partial_mats, "ta") / total_time
    for sweep in range(ITERS):
        basis = orthonormal(
            jnp.einsum("wcd,wdr->wcr", scatter_mat, basis, precision=lax.Precision.HIGHEST)
        )
    rounded = basis.astype(jnp.bfloat16)
    outputs = []
    for number in range(windows):
        frame = stacked[number * STRIDE : number * STRIDE + WIN]
        coeffs = jnp.dot(rounded[number].T, frame, preferred_element_type=jnp.float32).astype(
            jnp.bfloat16
        )
        fitted = jnp.dot(
            rounded[number, 2 * STRIDE : 3 * STRIDE], coeffs, preferred_element_type=jnp.float32
        )
        outputs.append(
            (frame[2 * STRIDE : 3 * STRIDE].astype(jnp.float32) - fitted).astype(jnp.bfloat16)
        )
    return jnp.concatenate(outputs, axis=0)


def solution(mesh):
    return jax.shard_map(
        per_device,
        mesh=mesh,
        in_specs=(P("ch", "ta"), P(), P()),
        out_specs=P("ch", "ta"),
        check_vma=False,
    )
```

profile of v0, /device:TPU:1, one launch (start us, length us, event | category | flops | bytes accessed | tf_op | source)
XLA Modules:
  0.0 292.5 jit_solution(11654293994104194249)
XLA Ops:
  7.7 10.2 %collective-permute-start = (bf16[256,64]{1,0:T(8,128)(2,1)S(1)}, bf16[256,64]{1,0:T(8,128)(2,1)S(1)}, u32[]{:S(2)}, u32[]{:S(2)}) collective-permute-start(bf16[256,64]{1,0:T(8,128)(2,1)S(1)} %get-tuple-element.10), channel_id=1, source_target_pairs={{0,1},{1,2},{2,3},{4,5},{5,6},{6,7},{8,9},{9,10},{10,11},{12,13},{... | collective-permute-start | bytes 98312 | tf_op jit(solution)/shard_map/ppermute | solution.py:20
  24.8 2.6 collective-permute-done.1
  32.8 4.0 %collective-permute-start.3 = (f32[4,5120]{1,0:T(4,128)S(1)}, f32[4,5120]{1,0:T(4,128)S(1)}, u32[]{:S(2)}, u32[]{:S(2)}) collective-permute-start(f32[4,5120]{1,0:T(4,128)S(1)} %bitcast.161), channel_id=1, source_target_pairs={{0,4},{4,8},{8,12},{12,16},{16,20},{20,24},{24,28},{28,32},{32,36}... | collective-permute-start | bytes 245768 | tf_op jit(solution)/shard_map/ppermute | solution.py:20
  36.8 5.9 %copy.21 = f32[256,20,256]{0,2,1:T(8,128)} copy(f32[256,20,256]{2,0,1:T(8,128)} %copy-done.3) | data formatting | bytes 10485760 | tf_op jit(solution)/shard_map/bct,tu->cbu/transpose | solution.py:60
  42.7 5.9 %copy.22 = f32[256,5120]{1,0:T(8,128)} copy(f32[256,5120]{0,1:T(8,128)} %bitcast.160) | data formatting | bytes 10485760 | tf_op jit(solution)/shard_map/reshape | solution.py:62
  48.6 4.7 %fusion.3 = bf16[256,5120]{1,0:T(8,128)(2,1)S(1)} fusion(f32[256,5120]{1,0:T(8,128)} %copy.22, f32[4,5120]{1,0:T(4,128)S(1)} %collective-permute-done.3, f32[4,5120]{1,0:T(4,128)S(1)} %collective-permute-done.2), kind=kLoop, calls=%fused_computation.10 | loop fusion | flops 5242880 | bytes 8028160 | tf_op jit(solution)/shard_map/convert_element_type | solution.py:64
  53.3 3.3 %collective-permute-start.4 = (bf16[256,5120]{1,0:T(8,128)(2,1)S(1)}, bf16[256,5120]{1,0:T(8,128)(2,1)S(1)}, u32[]{:S(2)}, u32[]{:S(2)}) collective-permute-start(bf16[256,5120]{1,0:T(8,128)(2,1)S(1)} %fusion.3), channel_id=1, source_target_pairs={{0,4},{4,8},{8,12},{12,16},{16,20},{20,24},{24,28},{28,32},{32,36}... | collective-permute-start | bytes 7864328 | tf_op jit(solution)/shard_map/ppermute | solution.py:31
  58.2 49.6 %collective-permute-done.4 = bf16[256,5120]{1,0:T(8,128)(2,1)S(1)} collective-permute-done((bf16[256,5120]{1,0:T(8,128)(2,1)S(1)}, bf16[256,5120]{1,0:T(8,128)(2,1)S(1)}, u32[]{:S(2)}, u32[]{:S(2)}) %collective-permute-start.4) | collective-permute-done | bytes 2621472 | tf_op jit(solution)/shard_map/ppermute | solution.py:31
  107.8 2.9 fusion.19
  110.8 2.9 fusion.18
  115.3 105.3 %all-reduce.3.cloned.1.call-done = f32[2,512,512]{2,1,0:T(8,128)} async-done(((f32[2,512,512]{2,1,0:T(8,128)}), f32[2,512,512]{2,1,0:T(8,128)}) %all-reduce.3.cloned.1.call-update) | async-done | bytes 2097168 | tf_op jit(solution)/shard_map/psum | solution.py:81
  220.6 3.6 %fusion.16 = f32[2,512,16]{1,2,0:T(8,128)S(1)} fusion(f32[2,512,512]{2,1,0:T(8,128)} %all-reduce.3.cloned.1.call-done, f32[512,16]{0,1:T(8,128)S(1)} %copy-done), kind=kOutput, calls=%fused_computation.28 | convolution fusion | flops 101187584 | bytes 2195456 | tf_op jit(solution)/shard_map/wcd,wdr->wcr/dot_general | solution.py:84
  224.5 3.1 %custom-call.16 = f32[2,16,16]{2,1,0:T(8,128)S(1)} custom-call(f32[2,16,16]{2,1,0:T(8,128)S(1)} %fusion.43), custom_call_target="Cholesky" | custom-call | tf_op jit(solution)/shard_map/jit(cholesky)/cholesky | solution.py:43
  227.8 2.5 custom-call.17
  230.6 3.5 %fusion.14 = f32[2,512,16]{1,2,0:T(8,128)S(1)} fusion(f32[2,512,16]{1,2,0:T(8,128)S(1)} %convolution_bitcast_fusion.6, f32[2,512,512]{2,1,0:T(8,128)} %all-reduce.3.cloned.1.call-done), kind=kOutput, calls=%fused_computation.26 | convolution fusion | flops 101187584 | bytes 2228224 | tf_op jit(solution)/shard_map/wcd,wdr->wcr/dot_general | solution.py:84
  234.4 2.9 %custom-call.18 = f32[2,16,16]{2,1,0:T(8,128)S(1)} custom-call(f32[2,16,16]{2,1,0:T(8,128)S(1)} %fusion.41), custom_call_target="Cholesky" | custom-call | tf_op jit(solution)/shard_map/jit(cholesky)/cholesky | solution.py:43
  242.5 2.9 %custom-call.20 = f32[2,16,16]{2,1,0:T(8,128)S(1)} custom-call(f32[2,16,16]{2,1,0:T(8,128)S(1)} %fusion.39), custom_call_target="Cholesky" | custom-call | tf_op jit(solution)/shard_map/jit(cholesky)/cholesky | solution.py:43
  250.7 2.9 %custom-call.22 = f32[2,16,16]{2,1,0:T(8,128)S(1)} custom-call(f32[2,16,16]{2,1,0:T(8,128)S(1)} %fusion.37), custom_call_target="Cholesky" | custom-call | tf_op jit(solution)/shard_map/jit(cholesky)/cholesky | solution.py:43
  258.8 2.9 %custom-call.24 = f32[2,16,16]{2,1,0:T(8,128)S(1)} custom-call(f32[2,16,16]{2,1,0:T(8,128)S(1)} %fusion.35), custom_call_target="Cholesky" | custom-call | tf_op jit(solution)/shard_map/jit(cholesky)/cholesky | solution.py:43
  266.9 2.9 %custom-call.26 = f32[2,16,16]{2,1,0:T(8,128)S(1)} custom-call(f32[2,16,16]{2,1,0:T(8,128)S(1)} %fusion.33), custom_call_target="Cholesky" | custom-call | tf_op jit(solution)/shard_map/jit(cholesky)/cholesky | solution.py:43
  270.1 2.6 custom-call.27
  273.0 5.3 %fusion = bf16[128,5120]{1,0:T(8,128)(2,1)} fusion(bf16[256,5120]{1,0:T(8,128)(2,1)} %copy-done.4, bf16[256,5120]{1,0:T(8,128)(2,1)} %copy-done.6, bf16[2,512,16]{1,2,0:T(8,128)(2,1)S(1)} %fusion.20), kind=kOutput, calls=%fused_computation.2 | convolution fusion | flops 117391360 | bytes 7884800 | tf_op jit(solution)/shard_map/dot_general | solution.py:93
  278.3 4.0 %fusion.1 = bf16[128,5120]{1,0:T(8,128)(2,1)} fusion(bf16[256,5120]{1,0:T(8,128)(2,1)S(1)} %copy-done.5, bf16[128,5120]{1,0:T(8,128)(2,1)} %copy-done.7, bf16[256,5120]{1,0:T(8,128)(2,1)} %copy-done.6, bf16[2,512,16]{1,2,0:T(8,128)(2,1)S(1)} %fusion.20), kind=kOutput, calls=%fused_computation.3 | convolution fusion | flops 122634240 | bytes 9195520 | tf_op jit(solution)/shard_map/dot_general | solution.py:93
  282.2 3.4 %pad_maximum_fusion.7 = bf16[256,5120]{1,0:T(8,128)(2,1)} fusion(bf16[128,5120]{1,0:T(8,128)(2,1)} %fusion.1, bf16[128,5120]{1,0:T(8,128)(2,1)} %fusion), kind=kLoop, calls=%fused_computation.14 | loop fusion | flops 5242880 | bytes 5242880 | tf_op jit(solution)/shard_map/concatenate | solution.py:99
  (107 shorter events, 38.7 us)
Async XLA Ops:
  6.5 214.0 %copy-start = (f32[512,16]{0,1:T(8,128)S(1)}, f32[512,16]{0,1:T(8,128)}, u32[]{:S(2)}) copy-start(f32[512,16]{0,1:T(8,128)} %param.8) | copy-start | bytes 98308
  6.5 15.7 %copy-start.2 = (bf16[256,5120]{1,0:T(8,128)(2,1)S(1)}, bf16[256,5120]{1,0:T(8,128)(2,1)}, u32[]{:S(2)}) copy-start(bf16[256,5120]{1,0:T(8,128)(2,1)} %param.6) | copy-start | bytes 7864324
  6.5 214.0 %all-reduce.3.cloned.1.call-start = ((), (), s32[]{:S(2)}) async-start(), calls=%async_computation | async-start | bytes 4194304 | tf_op jit(solution)/shard_map/psum | solution.py:81
  7.7 13.5 %collective-permute-start = (bf16[256,64]{1,0:T(8,128)(2,1)S(1)}, bf16[256,64]{1,0:T(8,128)(2,1)S(1)}, u32[]{:S(2)}, u32[]{:S(2)}) collective-permute-start(bf16[256,64]{1,0:T(8,128)(2,1)S(1)} %get-tuple-element.10), channel_id=1, source_target_pairs={{0,1},{1,2},{2,3},{4,5},{5,6},{6,7},{8,9},{9,10},{10,11},{12,13},{... | collective-permute-start | bytes 98312 | tf_op jit(solution)/shard_map/ppermute | solution.py:20
  17.9 9.5 %collective-permute-start.1 = (bf16[256,64]{1,0:T(8,128)(2,1)S(1)}, bf16[256,64]{1,0:T(8,128)(2,1)S(1)}, u32[]{:S(2)}, u32[]{:S(2)}) collective-permute-start(bf16[256,64]{1,0:T(8,128)(2,1)S(1)} %get-tuple-element.9), channel_id=1, source_target_pairs={{1,0},{2,1},{3,2},{5,4},{6,5},{7,6},{9,8},{10,9},{11,10},{13,12},{... | collective-permute-start | bytes 98312 | tf_op jit(solution)/shard_map/ppermute | solution.py:23
  29.1 2.3 copy-start.3
  31.5 17.2 %collective-permute-start.2 = (f32[4,5120]{1,0:T(4,128)S(1)}, f32[4,5120]{1,0:T(4,128)S(1)}, u32[]{:S(2)}, u32[]{:S(2)}) collective-permute-start(f32[4,5120]{1,0:T(4,128)S(1)} %bitcast.162), channel_id=1, source_target_pairs={{4,0},{8,4},{12,8},{16,12},{20,16},{24,20},{28,24},{32,28},{36,32}... | collective-permute-start | bytes 245768 | tf_op jit(solution)/shard_map/ppermute | solution.py:23
  32.8 15.9 %collective-permute-start.3 = (f32[4,5120]{1,0:T(4,128)S(1)}, f32[4,5120]{1,0:T(4,128)S(1)}, u32[]{:S(2)}, u32[]{:S(2)}) collective-permute-start(f32[4,5120]{1,0:T(4,128)S(1)} %bitcast.161), channel_id=1, source_target_pairs={{0,4},{4,8},{8,12},{12,16},{16,20},{20,24},{24,28},{28,32},{32,36}... | collective-permute-start | bytes 245768 | tf_op jit(solution)/shard_map/ppermute | solution.py:20
  53.3 57.4 %copy-start.4 = (bf16[256,5120]{1,0:T(8,128)(2,1)}, bf16[256,5120]{1,0:T(8,128)(2,1)S(1)}, u32[]{:S(2)}) copy-start(bf16[256,5120]{1,0:T(8,128)(2,1)S(1)} %fusion.3) | copy-start | bytes 7864324
  53.3 54.5 %collective-permute-start.4 = (bf16[256,5120]{1,0:T(8,128)(2,1)S(1)}, bf16[256,5120]{1,0:T(8,128)(2,1)S(1)}, u32[]{:S(2)}, u32[]{:S(2)}) collective-permute-start(bf16[256,5120]{1,0:T(8,128)(2,1)S(1)} %fusion.3), channel_id=1, source_target_pairs={{0,4},{4,8},{8,12},{12,16},{16,20},{20,24},{24,28},{28,32},{32,36}... | collective-permute-start | bytes 7864328 | tf_op jit(solution)/shard_map/ppermute | solution.py:31
  56.7 54.0 %collective-permute-start.5 = (bf16[128,5120]{1,0:T(8,128)(2,1)S(1)}, bf16[128,5120]{1,0:T(8,128)(2,1)S(1)}, u32[]{:S(2)}, u32[]{:S(2)}) collective-permute-start(bf16[128,5120]{1,0:T(8,128)(2,1)S(1)} %slice.168), channel_id=1, source_target_pairs={{4,0},{8,4},{12,8},{16,12},{20,16},{24,20},{28,24},{32,28},{36,32}... | collective-permute-start | bytes 3932168 | tf_op jit(solution)/shard_map/ppermute | solution.py:31
  107.8 2.9 %copy-start.6 = (bf16[256,5120]{1,0:T(8,128)(2,1)}, bf16[256,5120]{1,0:T(8,128)(2,1)S(1)}, u32[]{:S(2)}) copy-start(bf16[256,5120]{1,0:T(8,128)(2,1)S(1)} %collective-permute-done.4) | copy-start | bytes 7864324
  110.8 2.9 copy-start.7
  220.6 19.8 %copy-start.1 = (f32[2,512,512]{2,1,0:T(8,128)S(1)}, f32[2,512,512]{2,1,0:T(8,128)}, u32[]{:S(2)}) copy-start(f32[2,512,512]{2,1,0:T(8,128)} %all-reduce.3.cloned.1.call-done) | copy-start | bytes 6291460
  273.0 5.3 %copy-start.5 = (bf16[256,5120]{1,0:T(8,128)(2,1)S(1)}, bf16[256,5120]{1,0:T(8,128)(2,1)}, u32[]{:S(2)}) copy-start(bf16[256,5120]{1,0:T(8,128)(2,1)} %copy-done.4) | copy-start | bytes 7864324
Sparse Core Ops, SparseCore 0:
  115.4 105.1 all-reduce.2
where the time goes:
time: 293 us; the launch traced here: 292 us
  waiting for transfers between devices  158 us (54%)
  other arithmetic  45 us (15%)
  matrix products  34.3 us (12%)
  starting transfers between devices  22.2 us (8%)
  local copies, waits for them, and re-layouts  19.7 us (7%)
  between operations  13.8 us (5%)
    psum x1, waiting for transfers between devices, per_device(): scatter_mat = lax.psum(partial_mats, 'ta') / total_time  105 us
    ppermute x2, waiting for transfers between devices, shifted(): lax.ppermute(value, axis, [(source, source + steps) for source in range(f...  49.6 us
    another operation x19, other arithmetic, orthonormal(): lower = jnp.linalg.cholesky(gram)  18.7 us
    another operation x13, other arithmetic, orthonormal(): lax.linalg.triangular_solve(lower, image, left_side=False, lower=True, tr...  15.4 us
    dot_general x6, matrix products, per_device(): jnp.einsum('wcd,wdr->wcr', scatter_mat, basis, precision=lax.Precision.HI...  14.8 us
    ppermute x2, starting transfers between devices, with_halo(): lax.ppermute(lax.slice_in_dim(block, block.shape[dim] - width, None, axis...  14.2 us
    dot_general x2, matrix products, per_device(): jnp.dot(rounded[number, 2 * STRIDE:3 * STRIDE], coeffs, preferred_element...  9.23 us
    reshape x1, local copies, waits for them, and re-layouts, per_device(): filtered = jnp.einsum('bct,tu->cbu', pieces, band_matrix, preferred_eleme...  5.95 us
  transfers between devices with their start and end apart: 7, of which 3 were waited for; matrix products, arithmetic and copies ran while one was open for 7% of the time, Pallas kernels for 0%

commit v1 on v0

--- a/solution.py
+++ b/solution.py
@@ -78,7 +78,7 @@
             for number in range(windows)
         ]
     )
-    scatter_mat = lax.psum(partial_mats, "ta") / total_time
+    scatter_mat = jnp.sum(lax.all_gather(partial_mats, "ta"), axis=0) / total_time
     for sweep in range(ITERS):
         basis = orthonormal(
             jnp.einsum("wcd,wdr->wcr", scatter_mat, basis, precision=lax.Precision.HIGHEST)

time: 293 us -> 306 us (1.044)
  waiting for transfers between devices: 158 us -> 170 us
  other arithmetic: 45 us -> 49.6 us
  matrix products: 34.3 us -> 30.9 us
    all_gather x0 -> x1, waiting for transfers between devices: none -> 117 us  [per_device(): lax.all_gather(partial_mats, 'ta')]
    psum x1 -> x0, waiting for transfers between devices: 105 us -> none  [per_device(): scatter_mat = lax.psum(partial_mats, 'ta') / total_time]
    reduce_sum x0 -> x1, other arithmetic: none -> 4.65 us  [per_device(): jnp.sum(lax.all_gather(partial_mats, 'ta'), axis=0) / total_time]
    dot_general x6, matrix products: 14.8 us -> 11.4 us  [per_device(): jnp.einsum('wcd,wdr->wcr', scatter_mat, basis, precision=lax.Precision.HI...]
  transfers between devices with their start and end apart: 7 -> 7, of which waited for: 3 -> 3; matrix products, arithmetic and copies ran while one was open for 7% -> 6% of each run, Pallas kernels for 0% -> 0%
where the time goes in v1:
time: 306 us
  waiting for transfers between devices  170 us (56%)
  other arithmetic  49.6 us (16%)
  matrix products  30.9 us (10%)
  starting transfers between devices  22.2 us (7%)
  local copies, waits for them, and re-layouts  19.7 us (6%)
  between operations  13.8 us (5%)
    all_gather x1, waiting for transfers between devices, per_device(): lax.all_gather(partial_mats, 'ta')  117 us
    ppermute x2, waiting for transfers between devices, shifted(): lax.ppermute(value, axis, [(source, source + steps) for source in range(f...  49.6 us
    another operation x19, other arithmetic, orthonormal(): lower = jnp.linalg.cholesky(gram)  18.7 us
    another operation x13, other arithmetic, orthonormal(): lax.linalg.triangular_solve(lower, image, left_side=False, lower=True, tr...  15.4 us
    ppermute x2, starting transfers between devices, with_halo(): lax.ppermute(lax.slice_in_dim(block, block.shape[dim] - width, None, axis...  14.2 us
    dot_general x6, matrix products, per_device(): jnp.einsum('wcd,wdr->wcr', scatter_mat, basis, precision=lax.Precision.HI...  11.4 us
    dot_general x2, matrix products, per_device(): jnp.dot(rounded[number, 2 * STRIDE:3 * STRIDE], coeffs, preferred_element...  9.18 us
  transfers between devices with their start and end apart: 7, of which 3 were waited for; matrix products, arithmetic and copies ran while one was open for 6% of the time, Pallas kernels for 0%

profile of v1, /device:TPU:1, one launch (start us, length us, event | category | flops | bytes accessed | tf_op | source)
XLA Modules:
  0.0 305.9 jit_solution(10482147368269803812)
XLA Ops:
  7.7 10.2 %collective-permute-start = (bf16[256,64]{1,0:T(8,128)(2,1)S(1)}, bf16[256,64]{1,0:T(8,128)(2,1)S(1)}, u32[]{:S(2)}, u32[]{:S(2)}) collective-permute-start(bf16[256,64]{1,0:T(8,128)(2,1)S(1)} %get-tuple-element.10), channel_id=1, source_target_pairs={{0,1},{1,2},{2,3},{4,5},{5,6},{6,7},{8,9},{9,10},{10,11},{12,13},{... | collective-permute-start | bytes 98312 | tf_op jit(solution)/shard_map/ppermute | solution.py:20
  24.8 2.6 collective-permute-done.1
  32.8 4.0 %collective-permute-start.3 = (f32[4,5120]{1,0:T(4,128)S(1)}, f32[4,5120]{1,0:T(4,128)S(1)}, u32[]{:S(2)}, u32[]{:S(2)}) collective-permute-start(f32[4,5120]{1,0:T(4,128)S(1)} %bitcast.163), channel_id=1, source_target_pairs={{0,4},{4,8},{8,12},{12,16},{16,20},{20,24},{24,28},{28,32},{32,36}... | collective-permute-start | bytes 245768 | tf_op jit(solution)/shard_map/ppermute | solution.py:20
  36.8 5.9 %copy.36 = f32[256,20,256]{0,2,1:T(8,128)} copy(f32[256,20,256]{2,0,1:T(8,128)} %copy-done.2) | data formatting | bytes 10485760 | tf_op jit(solution)/shard_map/bct,tu->cbu/transpose | solution.py:60
  42.7 5.9 %copy.37 = f32[256,5120]{1,0:T(8,128)} copy(f32[256,5120]{0,1:T(8,128)} %bitcast.161) | data formatting | bytes 10485760 | tf_op jit(solution)/shard_map/reshape | solution.py:62
  48.6 4.7 %fusion.3 = bf16[256,5120]{1,0:T(8,128)(2,1)S(1)} fusion(f32[256,5120]{1,0:T(8,128)} %copy.37, f32[4,5120]{1,0:T(4,128)S(1)} %collective-permute-done.3, f32[4,5120]{1,0:T(4,128)S(1)} %collective-permute-done.2), kind=kLoop, calls=%fused_computation.10 | loop fusion | flops 5242880 | bytes 8028160 | tf_op jit(solution)/shard_map/convert_element_type | solution.py:64
  53.3 3.3 %collective-permute-start.4 = (bf16[256,5120]{1,0:T(8,128)(2,1)S(1)}, bf16[256,5120]{1,0:T(8,128)(2,1)S(1)}, u32[]{:S(2)}, u32[]{:S(2)}) collective-permute-start(bf16[256,5120]{1,0:T(8,128)(2,1)S(1)} %fusion.3), channel_id=1, source_target_pairs={{0,4},{4,8},{8,12},{12,16},{16,20},{20,24},{24,28},{28,32},{32,36}... | collective-permute-start | bytes 7864328 | tf_op jit(solution)/shard_map/ppermute | solution.py:31
  58.2 49.6 %collective-permute-done.4 = bf16[256,5120]{1,0:T(8,128)(2,1)S(1)} collective-permute-done((bf16[256,5120]{1,0:T(8,128)(2,1)S(1)}, bf16[256,5120]{1,0:T(8,128)(2,1)S(1)}, u32[]{:S(2)}, u32[]{:S(2)}) %collective-permute-start.4) | collective-permute-done | bytes 2621472 | tf_op jit(solution)/shard_map/ppermute | solution.py:31
  107.8 2.9 fusion.19
  110.8 2.9 fusion.18
  115.3 117.4 %all-gather.3.cloned.1.call-done = f32[8,512,512]{2,1,0:T(8,128)} async-done(((f32[2,512,512]{2,1,0:T(8,128)}), f32[8,512,512]{2,1,0:T(8,128)}) %all-gather.3.cloned.1.call-update) | async-done | bytes 8388624 | tf_op jit(solution)/shard_map/all_gather | solution.py:81
  232.7 4.7 %reduce_sum.9 = f32[2,512,512]{2,1,0:T(8,128)S(1)} reduce(f32[4,2,512,512]{3,2,1,0:T(8,128)} %bitcast.162, f32[]{:T(128)} %constant.35.clone.1), dimensions={0}, to_apply=%region_0.0 | reduce | flops 1572864 | bytes 10485764 | tf_op jit(solution)/shard_map/reduce_sum | solution.py:81
  239.6 3.1 %custom-call.16 = f32[2,16,16]{2,1,0:T(8,128)S(1)} custom-call(f32[2,16,16]{2,1,0:T(8,128)S(1)} %fusion.43), custom_call_target="Cholesky" | custom-call | tf_op jit(solution)/shard_map/jit(cholesky)/cholesky | solution.py:43
  242.9 2.5 custom-call.17
  247.8 2.9 custom-call.18
  256.0 2.9 custom-call.20
  264.1 2.9 custom-call.22
  267.3 2.5 custom-call.23
  272.2 2.9 custom-call.24
  280.4 2.9 custom-call.26
  283.6 2.6 custom-call.27
  286.5 5.3 %fusion = bf16[128,5120]{1,0:T(8,128)(2,1)} fusion(bf16[256,5120]{1,0:T(8,128)(2,1)} %copy-done.3, bf16[256,5120]{1,0:T(8,128)(2,1)} %copy-done.5, bf16[2,512,16]{1,2,0:T(8,128)(2,1)S(1)} %fusion.20), kind=kOutput, calls=%fused_computation.2 | convolution fusion | flops 117391360 | bytes 7884800 | tf_op jit(solution)/shard_map/dot_general | solution.py:93
  291.7 3.9 %fusion.1 = bf16[128,5120]{1,0:T(8,128)(2,1)} fusion(bf16[256,5120]{1,0:T(8,128)(2,1)S(1)} %copy-done.4, bf16[128,5120]{1,0:T(8,128)(2,1)} %copy-done.6, bf16[256,5120]{1,0:T(8,128)(2,1)} %copy-done.5, bf16[2,512,16]{1,2,0:T(8,128)(2,1)S(1)} %fusion.20), kind=kOutput, calls=%fused_computation.3 | convolution fusion | flops 122634240 | bytes 9195520 | tf_op jit(solution)/shard_map/dot_general | solution.py:93
  295.6 3.4 %pad_maximum_fusion.7 = bf16[256,5120]{1,0:T(8,128)(2,1)} fusion(bf16[128,5120]{1,0:T(8,128)(2,1)} %fusion.1, bf16[128,5120]{1,0:T(8,128)(2,1)} %fusion), kind=kLoop, calls=%fused_computation.14 | loop fusion | flops 5242880 | bytes 5242880 | tf_op jit(solution)/shard_map/concatenate | solution.py:99
  (106 shorter events, 40.0 us)
Async XLA Ops:
  6.5 230.8 %copy-start = (f32[512,16]{0,1:T(8,128)S(1)}, f32[512,16]{0,1:T(8,128)}, u32[]{:S(2)}) copy-start(f32[512,16]{0,1:T(8,128)} %param.8) | copy-start | bytes 98308
  6.5 15.7 %copy-start.1 = (bf16[256,5120]{1,0:T(8,128)(2,1)S(1)}, bf16[256,5120]{1,0:T(8,128)(2,1)}, u32[]{:S(2)}) copy-start(bf16[256,5120]{1,0:T(8,128)(2,1)} %param.6) | copy-start | bytes 7864324
  6.5 226.2 %all-gather.3.cloned.1.call-start = ((), (), s32[]{:S(2)}) async-start(), calls=%async_computation | async-start | bytes 10485760 | tf_op jit(solution)/shard_map/all_gather | solution.py:81
  7.7 13.5 %collective-permute-start = (bf16[256,64]{1,0:T(8,128)(2,1)S(1)}, bf16[256,64]{1,0:T(8,128)(2,1)S(1)}, u32[]{:S(2)}, u32[]{:S(2)}) collective-permute-start(bf16[256,64]{1,0:T(8,128)(2,1)S(1)} %get-tuple-element.10), channel_id=1, source_target_pairs={{0,1},{1,2},{2,3},{4,5},{5,6},{6,7},{8,9},{9,10},{10,11},{12,13},{... | collective-permute-start | bytes 98312 | tf_op jit(solution)/shard_map/ppermute | solution.py:20
  17.9 9.5 %collective-permute-start.1 = (bf16[256,64]{1,0:T(8,128)(2,1)S(1)}, bf16[256,64]{1,0:T(8,128)(2,1)S(1)}, u32[]{:S(2)}, u32[]{:S(2)}) collective-permute-start(bf16[256,64]{1,0:T(8,128)(2,1)S(1)} %get-tuple-element.9), channel_id=1, source_target_pairs={{1,0},{2,1},{3,2},{5,4},{6,5},{7,6},{9,8},{10,9},{11,10},{13,12},{... | collective-permute-start | bytes 98312 | tf_op jit(solution)/shard_map/ppermute | solution.py:23
  29.1 2.3 copy-start.2
  31.5 17.2 %collective-permute-start.2 = (f32[4,5120]{1,0:T(4,128)S(1)}, f32[4,5120]{1,0:T(4,128)S(1)}, u32[]{:S(2)}, u32[]{:S(2)}) collective-permute-start(f32[4,5120]{1,0:T(4,128)S(1)} %bitcast.164), channel_id=1, source_target_pairs={{4,0},{8,4},{12,8},{16,12},{20,16},{24,20},{28,24},{32,28},{36,32}... | collective-permute-start | bytes 245768 | tf_op jit(solution)/shard_map/ppermute | solution.py:23
  32.8 15.9 %collective-permute-start.3 = (f32[4,5120]{1,0:T(4,128)S(1)}, f32[4,5120]{1,0:T(4,128)S(1)}, u32[]{:S(2)}, u32[]{:S(2)}) collective-permute-start(f32[4,5120]{1,0:T(4,128)S(1)} %bitcast.163), channel_id=1, source_target_pairs={{0,4},{4,8},{8,12},{12,16},{16,20},{20,24},{24,28},{28,32},{32,36}... | collective-permute-start | bytes 245768 | tf_op jit(solution)/shard_map/ppermute | solution.py:20
  53.3 57.4 %copy-start.3 = (bf16[256,5120]{1,0:T(8,128)(2,1)}, bf16[256,5120]{1,0:T(8,128)(2,1)S(1)}, u32[]{:S(2)}) copy-start(bf16[256,5120]{1,0:T(8,128)(2,1)S(1)} %fusion.3) | copy-start | bytes 7864324
  53.3 54.5 %collective-permute-start.4 = (bf16[256,5120]{1,0:T(8,128)(2,1)S(1)}, bf16[256,5120]{1,0:T(8,128)(2,1)S(1)}, u32[]{:S(2)}, u32[]{:S(2)}) collective-permute-start(bf16[256,5120]{1,0:T(8,128)(2,1)S(1)} %fusion.3), channel_id=1, source_target_pairs={{0,4},{4,8},{8,12},{12,16},{16,20},{20,24},{24,28},{28,32},{32,36}... | collective-permute-start | bytes 7864328 | tf_op jit(solution)/shard_map/ppermute | solution.py:31
  56.7 54.0 %collective-permute-start.5 = (bf16[128,5120]{1,0:T(8,128)(2,1)S(1)}, bf16[128,5120]{1,0:T(8,128)(2,1)S(1)}, u32[]{:S(2)}, u32[]{:S(2)}) collective-permute-start(bf16[128,5120]{1,0:T(8,128)(2,1)S(1)} %slice.168), channel_id=1, source_target_pairs={{4,0},{8,4},{12,8},{16,12},{20,16},{24,20},{28,24},{32,28},{36,32}... | collective-permute-start | bytes 3932168 | tf_op jit(solution)/shard_map/ppermute | solution.py:31
  107.8 2.9 copy-start.5
  110.8 2.9 copy-start.6
  286.4 5.3 %copy-start.4 = (bf16[256,5120]{1,0:T(8,128)(2,1)S(1)}, bf16[256,5120]{1,0:T(8,128)(2,1)}, u32[]{:S(2)}) copy-start(bf16[256,5120]{1,0:T(8,128)(2,1)} %copy-done.3) | copy-start | bytes 7864324
Sparse Core Ops, SparseCore 0:
  115.4 117.3 all-gather.2
